TPU v7x, 32 devices: a whole 2x2x4 slice. The times are simulated.
32 devices in a mesh: dp: 8 (over y, x, core), tensor: 4 (over z).
Axes of the slice: x: 2, y: 2, z: 4, core: 2. Of those that a mesh axis runs over, the one named last changes fastest.
Arguments:
- teacher_master: float32 [256, 16384], P('dp', 'tensor'), as said below
- student_weight: bfloat16 [256, 16384], P('dp', 'tensor'), may hold values from -6 to 6
- teacher_feat: bfloat16 [2048, 256], P('dp'), as said below
- student_feat: bfloat16 [2048, 256], P('dp'), may hold values from -6 to 6
- center: float32 [16384], P('tensor'), may hold values from -0.3 to 0.3
Outputs:
- master_new: float32 [256, 16384], P('dp', 'tensor')
- student_grad: float32 [256, 16384], P('dp', 'tensor')
- new_center: float32 [16384], P('tensor')
Inputs may be any that keep to these rules, and one draw needn't show every extreme that they name: `teacher_feat`: rows of teacher features are real-valued and of order one. `teacher_master`: entries of the teacher master are real-valued and of order one.
All inputs are finite; a program needn't handle non-finite values.
Results may differ from a plain program's by a relative error of at most 0.014.
Values may be sent and summed in bfloat16 or wider, within the bound.
No kernel may reach another device: no remote copies, remote signals or barrier semaphores. Data moves between devices by JAX's collectives and lax.ppermute only.
A program may use at most 64 MiB of HBM per device.

v0:
```python
import jax
import jax.numpy as jnp
from jax import lax
from jax.sharding import PartitionSpec as P


def unit_rows(feat):
    wide = feat.astype(jnp.float32)
    return (wide * lax.rsqrt(jnp.sum(wide * wide, 1, keepdims=True) + 1e-06)).astype(jnp.bfloat16)


def shards(teacher_master, student_weight, teacher_feat, student_feat, center):
    zt = unit_rows(teacher_feat)
    zs = unit_rows(student_feat)
    images_all = teacher_feat.shape[0] * lax.axis_size("dp")
    student_full = lax.all_gather(student_weight, "dp", axis=0, tiled=True)
    master_new = 0.996 * teacher_master + 0.004 * student_weight.astype(jnp.float32)
    weight = lax.all_gather(master_new.astype(jnp.bfloat16), "dp", axis=0, tiled=True)
    feats = zt
    raw = jnp.dot(feats, weight, preferred_element_type=jnp.float32)
    squares = jnp.sum(jnp.square(weight.astype(jnp.float32)), 0)
    t_norm = jnp.sqrt(squares + 1e-06)
    t_cos = raw / t_norm
    s_norm = jnp.sqrt(jnp.sum(jnp.square(student_full.astype(jnp.float32)), 0) + 1e-06)
    s_cos = jnp.dot(zs, student_full, preferred_element_type=jnp.float32) / s_norm
    t_exp = jnp.exp((t_cos - center) / 0.04)
    s_exp = jnp.exp(s_cos / 0.1)
    t_total, s_total = lax.psum(
        (jnp.sum(t_exp, 1, keepdims=True), jnp.sum(s_exp, 1, keepdims=True)), "tensor"
    )
    cos_mean = lax.psum(jnp.sum(t_cos, 0), "dp") / images_all
    new_center = 0.5 * center + 0.5 * cos_mean
    dlog = ((s_exp / s_total - t_exp / t_total) / 0.1).astype(jnp.bfloat16)
    weighted = jnp.sum(dlog.astype(jnp.float32) * s_cos, 0)
    scaled = weighted / s_norm
    feats = zs
    product = lax.dot_general(
        feats, dlog, (((0,), (0,)), ((), ())), preferred_element_type=jnp.float32
    )
    student_grad = lax.psum_scatter(
        (product - student_full.astype(jnp.float32) * scaled) / s_norm,
        "dp",
        scatter_dimension=0,
        tiled=True,
    )
    return (master_new, student_grad, new_center)


def solution(mesh):
    placed = (P("dp", "tensor"), P("dp", "tensor"), P("dp", None), P("dp", None), P("tensor"))
    return jax.shard_map(
        shards,
        mesh=mesh,
        in_specs=placed,
        out_specs=(P("dp", "tensor"), P("dp", "tensor"), P("tensor")),
        check_vma=False,
    )
```

profile of v0, /device:TPU:0, one launch (start us, length us, event | category | flops | bytes accessed | tf_op | source)
XLA Modules:
  0.0 153.8 jit_solution(11268141412257356897)
XLA Ops:
  7.2 0.0 copy-start.3
  7.2 0.0 all-gather.3.cloned.1.call-start
  7.2 0.7 all-gather.3.cloned.1.call-update
  7.9 0.0 all-gather.5.cloned.1.call-start
  8.0 2.1 %fusion.13 = (bf16[32,4096]{1,0:T(8,128)(2,1)}, f32[32,4096]{1,0:T(8,128)}) fusion(bf16[32,4096]{1,0:T(8,128)(2,1)} %param.6, f32[32,4096]{1,0:T(8,128)} %param.5), kind=kLoop, calls=%fused_computation.31 | loop fusion | flops 655360 | bytes 1572864 | tf_op jit(solution)/shard_map/convert_element_type | solution.py:18
  10.0 0.0 all-gather.5.cloned.1.call-update
  10.1 0.0 reduce-scatter.2.cloned.1.call-start
  10.1 1.0 fusion.6
  11.1 1.0 fusion.4
  12.2 28.3 %all-gather.3.cloned.1.call-done = bf16[256,4096]{1,0:T(8,128)(2,1)} async-done(((bf16[32,4096]{1,0:T(8,128)(2,1)}), bf16[256,4096]{1,0:T(8,128)(2,1)}) %all-gather.3.cloned.1.call-update) | async-done | bytes 2097168 | tf_op jit(solution)/shard_map/all_gather | solution.py:16
  40.5 0.0 copy-start
  40.5 2.2 %fusion.1 = f32[4096]{0:T(1024)S(1)} fusion(bf16[256,4096]{1,0:T(8,128)(2,1)} %all-gather.3.cloned.1.call-done), kind=kLoop, calls=%fused_computation.6 | loop fusion | flops 3141632 | bytes 2113536 | tf_op jit(solution)/shard_map/reduce_sum | solution.py:24
  42.7 28.2 %all-gather.5.cloned.1.call-done = bf16[256,4096]{1,0:T(8,128)(2,1)} async-done(((bf16[32,4096]{1,0:T(8,128)(2,1)}), bf16[256,4096]{1,0:T(8,128)(2,1)}) %all-gather.5.cloned.1.call-update) | async-done | bytes 2097168 | tf_op jit(solution)/shard_map/all_gather | solution.py:18
  70.9 2.0 %multiply_reduce_fusion.1 = f32[4096]{0:T(1024)S(1)} fusion(bf16[256,4096]{1,0:T(8,128)(2,1)} %all-gather.5.cloned.1.call-done), kind=kLoop, calls=%fused_computation.10 | loop fusion | flops 3141632 | bytes 2113536 | tf_op jit(solution)/shard_map/reduce_sum | solution.py:21
  73.0 0.0 copy-done.3
  73.0 0.0 copy-done
  73.0 0.0 copy-start.1
  73.0 0.0 copy-start.2
  73.0 0.0 copy-start.4
  73.0 3.1 %fusion.2 = (f32[256]{0:T(256)S(1)}, f32[256,4096]{1,0:T(8,128)}) fusion(f32[4096]{0:T(1024)S(1)} %add_sqrt_fusion.1, bf16[256,4096]{1,0:T(8,128)(2,1)S(1)} %copy-done, bf16[256,256]{1,0:T(8,128)(2,1)S(1)} %copy-done.3, f32[256]{0:T(256)S(1)} %add_rsqrt_fusion.1), kind=kOutput, calls=%fused_computation.12 | convolution fusion | flops 540212992 | bytes 6440960 | tf_op jit(solution)/shard_map/dot_general | solution.py:25
  76.1 0.0 copy-done.1
  76.1 0.0 copy-done.2
  76.1 0.0 copy-done.4
  76.1 3.4 %fusion.12 = (f32[4096]{0:T(1024)S(1)}, f32[256]{0:T(256)S(1)}, f32[256,4096]{1,0:T(8,128)}) fusion(f32[4096]{0:T(1024)S(1)} %copy-done.4, f32[4096]{0:T(1024)S(1)} %add_sqrt_fusion, bf16[256,4096]{1,0:T(8,128)(2,1)S(1)} %copy-done.1, bf16[256,256]{1,0:T(8,128)(2,1)S(1)} %copy-done.2, f32[256]{0:T(256)S(1)} %add_rsqrt_fusion), kind=kOutput, calls=%fused_computation.30 | convolution fusion | flops 542306048 | bytes 6473728 | tf_op jit(solution)/shard_map/dot_general | solution.py:20
  79.5 11.7 %all-reduce = (f32[256]{0:T(256)S(1)}, f32[256]{0:T(256)S(1)}) all-reduce(f32[256]{0:T(256)S(1)} %get-tuple-element.4, f32[256]{0:T(256)S(1)} %get-tuple-element.12), channel_id=1, replica_groups=mesh['dp'=8,'tensor'=4] {'tensor'}, use_global_device_ids=true, to_apply=%region_7.0 | all-reduce | flops 512 | bytes 4096 | tf_op jit(solution)/shard_map/psum | solution.py:28
  91.1 4.5 %multiply_reduce_fusion = (f32[4096]{0:T(1024)S(1)}, bf16[256,4096]{1,0:T(8,128)(2,1)S(1)}) fusion(f32[256,4096]{1,0:T(8,128)} %get-tuple-element.13, f32[256]{0:T(256)S(1)} %get-tuple-element.5, f32[256,4096]{1,0:T(8,128)} %get-tuple-element.11, f32[4096]{0:T(1024)S(1)} %copy-done.4, f32[256]{0:T(256)S(1)} %get-tuple-element.6), kind=kLoop, calls=%fused_computation.7 | loop fusion | flops 11530240 | bytes 10520576 | tf_op jit(solution)/shard_map/reduce_sum | solution.py:34
  95.6 3.0 %fusion = f32[256,4096]{1,0:T(8,128)} fusion(bf16[256,4096]{1,0:T(8,128)(2,1)S(1)} %get-tuple-element.8, bf16[256,4096]{1,0:T(8,128)(2,1)S(1)} %copy-done, f32[4096]{0:T(1024)S(1)} %rsqrt_multiply_fusion, f32[4096]{0:T(1024)S(1)} %add_sqrt_fusion.1, bf16[256,256]{1,0:T(8,128)(2,1)S(1)} %copy-done.3, f32[256]{0:T(256)S(1)} %add_rsqrt_fusion.1), kind=kOutput, calls=%fused_computation.5 | convolution fusion | flops 541261824 | bytes 8553472 | tf_op jit(solution)/shard_map/dot_general | solution.py:37
  98.6 0.0 reduce-scatter.2.cloned.1.call-update
  98.6 22.4 %psum.23 = f32[4096]{0:T(1024)S(1)} all-reduce(f32[4096]{0:T(1024)S(1)} %get-tuple-element.3), channel_id=1, replica_groups=mesh['dp'=8,'tensor'=4] {'dp'}, use_global_device_ids=true, to_apply=%region_11.0 | all-reduce | flops 4096 | bytes 32768 | tf_op jit(solution)/shard_map/psum | solution.py:31
  121.0 0.6 multiply_add_fusion.1
  121.6 25.7 %reduce-scatter.2.cloned.1.call-done = f32[32,4096]{1,0:T(8,128)} async-done(((f32[256,4096]{1,0:T(8,128)}), f32[32,4096]{1,0:T(8,128)}) %reduce-scatter.2.cloned.1.call-update) | async-done | bytes 524304 | tf_op jit(solution)/shard_map/reduce_scatter | solution.py:40
  (5 shorter events, 0.0 us)
Async XLA Ops:
  7.2 65.8 %copy-start.3 = (bf16[256,256]{1,0:T(8,128)(2,1)S(1)}, bf16[256,256]{1,0:T(8,128)(2,1)}, u32[]{:S(2)}) copy-start(bf16[256,256]{1,0:T(8,128)(2,1)} %param.8) | copy-start | bytes 393220
  7.2 33.4 %all-gather.3.cloned.1.call-start = ((), (), s32[]{:S(2)}) async-start(), calls=%async_computation.1 | async-start | bytes 2359296 | tf_op jit(solution)/shard_map/all_gather | solution.py:16
  7.9 63.0 %all-gather.5.cloned.1.call-start = ((), (), s32[]{:S(2)}) async-start(), calls=%async_computation.2 | async-start | bytes 2359296 | tf_op jit(solution)/shard_map/all_gather | solution.py:18
  10.1 137.2 %reduce-scatter.2.cloned.1.call-start = ((), (), s32[]{:S(2)}) async-start(), calls=%async_computation.3 | async-start | bytes 4718592 | tf_op jit(solution)/shard_map/reduce_scatter | solution.py:40
  40.5 32.5 %copy-start = (bf16[256,4096]{1,0:T(8,128)(2,1)S(1)}, bf16[256,4096]{1,0:T(8,128)(2,1)}, u32[]{:S(2)}) copy-start(bf16[256,4096]{1,0:T(8,128)(2,1)} %all-gather.3.cloned.1.call-done) | copy-start | bytes 6291460
  73.0 3.1 %copy-start.1 = (bf16[256,4096]{1,0:T(8,128)(2,1)S(1)}, bf16[256,4096]{1,0:T(8,128)(2,1)}, u32[]{:S(2)}) copy-start(bf16[256,4096]{1,0:T(8,128)(2,1)} %all-gather.5.cloned.1.call-done) | copy-start | bytes 6291460
  73.0 3.1 %copy-start.2 = (bf16[256,256]{1,0:T(8,128)(2,1)S(1)}, bf16[256,256]{1,0:T(8,128)(2,1)}, u32[]{:S(2)}) copy-start(bf16[256,256]{1,0:T(8,128)(2,1)} %param.7) | copy-start | bytes 393220
  73.0 3.1 %copy-start.4 = (f32[4096]{0:T(1024)S(1)}, f32[4096]{0:T(1024)}, u32[]{:S(2)}) copy-start(f32[4096]{0:T(1024)} %param.9) | copy-start | bytes 49156
Sparse Core Ops, SparseCore 0:
  9.9 30.5 all-gather.2
  43.0 27.8 all-gather.4
  98.7 48.5 reduce-scatter.1
where the time goes:
time: 154 us
  waiting for transfers between devices  82.9 us (54%)
  blocking collectives  34.1 us (22%)
  between operations  13.9 us (9%)
  other arithmetic  13.4 us (9%)
  matrix products  9.39 us (6%)
    all_gather x1, waiting for transfers between devices, shards(): student_full = lax.all_gather(student_weight, 'dp', axis=0, tiled=True)  28.3 us
    all_gather x1, waiting for transfers between devices, shards(): lax.all_gather(master_new.astype(jnp.bfloat16), 'dp', axis=0, tiled=True)  28.2 us
    reduce_scatter x1, waiting for transfers between devices, shards(): lax.psum_scatter((product - student_full.astype(jnp.float32) * scaled) /...  25.7 us
    psum x1, blocking collectives, shards(): cos_mean = lax.psum(jnp.sum(t_cos, 0), 'dp') / images_all  22.4 us
    psum x1, blocking collectives, shards(): lax.psum((jnp.sum(t_exp, 1, keepdims=True), jnp.sum(s_exp, 1, keepdims=Tr...  11.7 us
    reduce_sum x1, other arithmetic, shards(): weighted = jnp.sum(dlog.astype(jnp.float32) * s_cos, 0)  4.47 us
    dot_general x1, matrix products, shards(): raw = jnp.dot(feats, weight, preferred_element_type=jnp.float32)  3.37 us
  transfers between devices with their start and end apart: 3, of which 3 were waited for; matrix products, arithmetic and copies ran while one was open for 5% of the time, Pallas kernels for 0%

commit v1 on v0

--- a/solution.py
+++ b/solution.py
@@ -2,6 +2,19 @@
 import jax.numpy as jnp
 from jax import lax
 from jax.sharding import PartitionSpec as P
+
+
+def collect(x, axis, dim):
+    devices, index, extent = (lax.axis_size(axis), lax.axis_index(axis), x.shape[dim])
+    right = [(i, (i + 1) % devices) for i in range(devices)]
+    out = jnp.zeros((*x.shape[:dim], devices * extent, *x.shape[dim + 1 :]), x.dtype)
+    held = x
+    for turn in range(devices):
+        owner = (index - turn) % devices
+        out = lax.dynamic_update_slice_in_dim(out, held, owner * extent, axis=dim)
+        if turn < devices - 1:
+            held = lax.ppermute(held, axis, right)
+    return out
 
 
 def unit_rows(feat):
@@ -13,7 +26,7 @@
     zt = unit_rows(teacher_feat)
     zs = unit_rows(student_feat)
     images_all = teacher_feat.shape[0] * lax.axis_size("dp")
-    student_full = lax.all_gather(student_weight, "dp", axis=0, tiled=True)
+    student_full = collect(student_weight, "dp", 0)
     master_new = 0.996 * teacher_master + 0.004 * student_weight.astype(jnp.float32)
     weight = lax.all_gather(master_new.astype(jnp.bfloat16), "dp", axis=0, tiled=True)
     feats = zt

time: 154 us -> 144 us (0.935)
  waiting for transfers between devices: 82.9 us -> 73.1 us
  other arithmetic: 13.4 us -> 10.8 us
  matrix products: 9.39 us -> 11 us
    ppermute x0 -> x7, waiting for transfers between devices: none -> 46.7 us  [collect(): held = lax.ppermute(held, axis, right)]
    all_gather x1 -> x0, waiting for transfers between devices: 28.3 us -> none  [shards(): student_full = lax.all_gather(student_weight, 'dp', axis=0, tiled=True)]
    all_gather x1, waiting for transfers between devices: 28.2 us -> 0.01 us  [shards(): lax.all_gather(master_new.astype(jnp.bfloat16), 'dp', axis=0, tiled=True)]
    reduce_sum x1, other arithmetic: 2.18 us -> 0.44 us  [shards(): jnp.sum(jnp.square(student_full.astype(jnp.float32)), 0) + 1e-06]
    dot_general x1, matrix products: 3.37 us -> 4.94 us  [shards(): raw = jnp.dot(feats, weight, preferred_element_type=jnp.float32)]
  transfers between devices with their start and end apart: 3 -> 9, of which waited for: 3 -> 8; matrix products, arithmetic and copies ran while one was open for 5% -> 5% of each run, Pallas kernels for 0% -> 0%
where the time goes in v1:
time: 144 us
  waiting for transfers between devices  73.1 us (51%)
  blocking collectives  34 us (24%)
  between operations  14.4 us (10%)
  matrix products  11 us (8%)
  other arithmetic  10.8 us (8%)
    ppermute x7, waiting for transfers between devices, collect(): held = lax.ppermute(held, axis, right)  46.7 us
    reduce_scatter x1, waiting for transfers between devices, shards(): lax.psum_scatter((product - student_full.astype(jnp.float32) * scaled) /...  26.3 us
    psum x1, blocking collectives, shards(): cos_mean = lax.psum(jnp.sum(t_cos, 0), 'dp') / images_all  22.3 us
    psum x1, blocking collectives, shards(): lax.psum((jnp.sum(t_exp, 1, keepdims=True), jnp.sum(s_exp, 1, keepdims=Tr...  11.7 us
    dot_general x1, matrix products, shards(): raw = jnp.dot(feats, weight, preferred_element_type=jnp.float32)  4.94 us
    reduce_sum x1, other arithmetic, shards(): weighted = jnp.sum(dlog.astype(jnp.float32) * s_cos, 0)  4.47 us
    dot_general x1, matrix products, shards(): jnp.dot(zs, student_full, preferred_element_type=jnp.float32) / s_norm  3.06 us
    dot_general x1, matrix products, shards(): lax.dot_general(feats, dlog, (((0,), (0,)), ((), ())), preferred_element_...  2.95 us
  transfers between devices with their start and end apart: 9, of which 8 were waited for; matrix products, arithmetic and copies ran while one was open for 5% of the time, Pallas kernels for 0%

profile of v1, /device:TPU:0, one launch (start us, length us, event | category | flops | bytes accessed | tf_op | source)
XLA Modules:
  0.0 144.2 jit_solution(6435399175421276920)
XLA Ops:
  7.2 0.0 all-gather.2.cloned.1.call-start
  7.2 0.5 collective-permute-start
  7.7 2.1 %fusion.17 = (bf16[32,4096]{1,0:T(8,128)(2,1)}, f32[32,4096]{1,0:T(8,128)}) fusion(bf16[32,4096]{1,0:T(8,128)(2,1)} %param.6, f32[32,4096]{1,0:T(8,128)} %param.5), kind=kLoop, calls=%fused_computation.40 | loop fusion | flops 655360 | bytes 1572864 | tf_op jit(solution)/shard_map/convert_element_type | solution.py:31
  9.8 0.0 all-gather.2.cloned.1.call-update
  9.8 0.0 reduce-scatter.2.cloned.1.call-start
  9.9 1.0 fusion.7
  10.9 0.2 broadcast_in_dim.6
  11.2 0.1 fusion.5
  11.5 3.4 %collective-permute-done = bf16[32,4096]{1,0:T(8,128)(2,1)S(1)} collective-permute-done((bf16[32,4096]{1,0:T(8,128)(2,1)}, bf16[32,4096]{1,0:T(8,128)(2,1)S(1)}, u32[]{:S(2)}, u32[]{:S(2)}) %collective-permute-start) | collective-permute-done | bytes 262176 | tf_op jit(solution)/shard_map/ppermute | solution.py:16
  14.9 0.0 collective-permute-start.1
  14.9 6.7 %collective-permute-done.1 = bf16[32,4096]{1,0:T(8,128)(2,1)S(1)} collective-permute-done((bf16[32,4096]{1,0:T(8,128)(2,1)S(1)}, bf16[32,4096]{1,0:T(8,128)(2,1)S(1)}, u32[]{:S(2)}, u32[]{:S(2)}) %collective-permute-start.1) | collective-permute-done | bytes 262176 | tf_op jit(solution)/shard_map/ppermute | solution.py:16
  21.6 0.0 collective-permute-start.2
  21.6 8.2 %collective-permute-done.2 = bf16[32,4096]{1,0:T(8,128)(2,1)S(1)} collective-permute-done((bf16[32,4096]{1,0:T(8,128)(2,1)S(1)}, bf16[32,4096]{1,0:T(8,128)(2,1)S(1)}, u32[]{:S(2)}, u32[]{:S(2)}) %collective-permute-start.2) | collective-permute-done | bytes 262176 | tf_op jit(solution)/shard_map/ppermute | solution.py:16
  29.8 0.0 collective-permute-start.3
  29.8 8.5 %collective-permute-done.3 = bf16[32,4096]{1,0:T(8,128)(2,1)S(1)} collective-permute-done((bf16[32,4096]{1,0:T(8,128)(2,1)S(1)}, bf16[32,4096]{1,0:T(8,128)(2,1)S(1)}, u32[]{:S(2)}, u32[]{:S(2)}) %collective-permute-start.3) | collective-permute-done | bytes 262176 | tf_op jit(solution)/shard_map/ppermute | solution.py:16
  38.3 0.0 collective-permute-start.4
  38.3 6.7 %collective-permute-done.4 = bf16[32,4096]{1,0:T(8,128)(2,1)S(1)} collective-permute-done((bf16[32,4096]{1,0:T(8,128)(2,1)S(1)}, bf16[32,4096]{1,0:T(8,128)(2,1)S(1)}, u32[]{:S(2)}, u32[]{:S(2)}) %collective-permute-start.4) | collective-permute-done | bytes 262176 | tf_op jit(solution)/shard_map/ppermute | solution.py:16
  45.0 6.7 %collective-permute-done.5 = bf16[32,4096]{1,0:T(8,128)(2,1)S(1)} collective-permute-done((bf16[32,4096]{1,0:T(8,128)(2,1)S(1)}, bf16[32,4096]{1,0:T(8,128)(2,1)S(1)}, u32[]{:S(2)}, u32[]{:S(2)}) %collective-permute-start.5) | collective-permute-done | bytes 262176 | tf_op jit(solution)/shard_map/ppermute | solution.py:16
  51.7 6.7 %collective-permute-done.6 = bf16[32,4096]{1,0:T(8,128)(2,1)S(1)} collective-permute-done((bf16[32,4096]{1,0:T(8,128)(2,1)S(1)}, bf16[32,4096]{1,0:T(8,128)(2,1)S(1)}, u32[]{:S(2)}, u32[]{:S(2)}) %collective-permute-start.6) | collective-permute-done | bytes 262176 | tf_op jit(solution)/shard_map/ppermute | solution.py:16
  58.4 0.4 fusion
  58.9 0.0 copy-start.1
  58.9 0.0 copy-start.3
  58.9 3.1 %fusion.3 = (f32[256]{0:T(256)S(1)}, f32[256,4096]{1,0:T(8,128)}) fusion(f32[4096]{0:T(1024)S(1)} %add_sqrt_fusion.1, bf16[256,4096]{1,0:T(8,128)(2,1)S(1)} %constant_dynamic-update-slice_fusion, bf16[256,256]{1,0:T(8,128)(2,1)S(1)} %copy-done.2, f32[256]{0:T(256)S(1)} %add_rsqrt_fusion.1), kind=kOutput, calls=%fused_computation.12 | convolution fusion | flops 540212992 | bytes 6440960 | tf_op jit(solution)/shard_map/dot_general | solution.py:38
  62.0 2.0 %multiply_reduce_fusion.1 = f32[4096]{0:T(1024)S(1)} fusion(bf16[256,4096]{1,0:T(8,128)(2,1)} %all-gather.2.cloned.1.call-done), kind=kLoop, calls=%fused_computation.10 | loop fusion | flops 3141632 | bytes 2113536 | tf_op jit(solution)/shard_map/reduce_sum | solution.py:34
  64.0 4.9 %fusion.16 = (f32[4096]{0:T(1024)S(1)}, f32[256]{0:T(256)S(1)}, f32[256,4096]{1,0:T(8,128)}) fusion(f32[4096]{0:T(1024)S(1)} %copy-done.3, f32[4096]{0:T(1024)S(1)} %add_sqrt_fusion, bf16[256,4096]{1,0:T(8,128)(2,1)} %all-gather.2.cloned.1.call-done, bf16[256,256]{1,0:T(8,128)(2,1)S(1)} %copy-done.1, f32[256]{0:T(256)S(1)} %add_rsqrt_fusion), kind=kOutput, calls=%fused_computation.39 | convolution fusion | flops 542306048 | bytes 6473728 | tf_op jit(solution)/shard_map/dot_general | solution.py:33
  69.0 11.7 %all-reduce = (f32[256]{0:T(256)S(1)}, f32[256]{0:T(256)S(1)}) all-reduce(f32[256]{0:T(256)S(1)} %get-tuple-element.4, f32[256]{0:T(256)S(1)} %get-tuple-element.12), channel_id=1, replica_groups=mesh['dp'=8,'tensor'=4] {'tensor'}, use_global_device_ids=true, to_apply=%region_7.8 | all-reduce | flops 512 | bytes 4096 | tf_op jit(solution)/shard_map/psum | solution.py:41
  80.6 4.5 %multiply_reduce_fusion = (f32[4096]{0:T(1024)S(1)}, bf16[256,4096]{1,0:T(8,128)(2,1)S(1)}) fusion(f32[256,4096]{1,0:T(8,128)} %get-tuple-element.13, f32[256]{0:T(256)S(1)} %get-tuple-element.5, f32[256,4096]{1,0:T(8,128)} %get-tuple-element.11, f32[4096]{0:T(1024)S(1)} %copy-done.3, f32[256]{0:T(256)S(1)} %get-tuple-element.6), kind=kLoop, calls=%fused_computation.7 | loop fusion | flops 11530240 | bytes 10520576 | tf_op jit(solution)/shard_map/reduce_sum | solution.py:47
  85.1 3.0 %fusion.2 = f32[256,4096]{1,0:T(8,128)} fusion(bf16[256,4096]{1,0:T(8,128)(2,1)S(1)} %constant_dynamic-update-slice_fusion, f32[4096]{0:T(1024)S(1)} %rsqrt_multiply_fusion, f32[4096]{0:T(1024)S(1)} %add_sqrt_fusion.1, bf16[256,4096]{1,0:T(8,128)(2,1)S(1)} %get-tuple-element.8, bf16[256,256]{1,0:T(8,128)(2,1)S(1)} %copy-done.2, f32[256]{0:T(256)S(1)} %add_rsqrt_fusion.1), kind=kOutput, calls=%fused_computation.6 | convolution fusion | flops 541261824 | bytes 8553472 | tf_op jit(solution)/shard_map/dot_general | solution.py:50
  88.1 0.0 reduce-scatter.2.cloned.1.call-update
  88.1 22.3 %psum.23 = f32[4096]{0:T(1024)S(1)} all-reduce(f32[4096]{0:T(1024)S(1)} %get-tuple-element.3), channel_id=1, replica_groups=mesh['dp'=8,'tensor'=4] {'dp'}, use_global_device_ids=true, to_apply=%region_11.12 | all-reduce | flops 4096 | bytes 32768 | tf_op jit(solution)/shard_map/psum | solution.py:44
  110.4 0.6 multiply_add_fusion.1
  111.0 26.3 %reduce-scatter.2.cloned.1.call-done = f32[32,4096]{1,0:T(8,128)} async-done(((f32[256,4096]{1,0:T(8,128)}), f32[32,4096]{1,0:T(8,128)}) %reduce-scatter.2.cloned.1.call-update) | async-done | bytes 524304 | tf_op jit(solution)/shard_map/reduce_scatter | solution.py:53
  (22 shorter events, 0.2 us)
Async XLA Ops:
  7.2 4.0 %copy-start = (bf16[32,4096]{1,0:T(8,128)(2,1)S(1)}, bf16[32,4096]{1,0:T(8,128)(2,1)}, u32[]{:S(2)}) copy-start(bf16[32,4096]{1,0:T(8,128)(2,1)} %param.6) | copy-start | bytes 786436
  7.2 4.1 %copy-start.2 = (bf16[256,256]{1,0:T(8,128)(2,1)S(1)}, bf16[256,256]{1,0:T(8,128)(2,1)}, u32[]{:S(2)}) copy-start(bf16[256,256]{1,0:T(8,128)(2,1)} %param.8) | copy-start | bytes 393220
  7.2 54.8 %all-gather.2.cloned.1.call-start = ((), (), s32[]{:S(2)}) async-start(), calls=%async_computation.1 | async-start | bytes 2359296 | tf_op jit(solution)/shard_map/all_gather | solution.py:31
  7.2 7.7 %collective-permute-start = (bf16[32,4096]{1,0:T(8,128)(2,1)}, bf16[32,4096]{1,0:T(8,128)(2,1)S(1)}, u32[]{:S(2)}, u32[]{:S(2)}) collective-permute-start(bf16[32,4096]{1,0:T(8,128)(2,1)} %param.6), channel_id=1, source_target_pairs={{0,4},{4,8},{8,12},{12,16},{16,20},{20,24},{24,28},{28,0},{1,5},{5... | collective-permute-start | bytes 786440 | tf_op jit(solution)/shard_map/ppermute | solution.py:16
  9.8 127.5 %reduce-scatter.2.cloned.1.call-start = ((), (), s32[]{:S(2)}) async-start(), calls=%async_computation.2 | async-start | bytes 4718592 | tf_op jit(solution)/shard_map/reduce_scatter | solution.py:53
  14.9 6.7 %collective-permute-start.1 = (bf16[32,4096]{1,0:T(8,128)(2,1)S(1)}, bf16[32,4096]{1,0:T(8,128)(2,1)S(1)}, u32[]{:S(2)}, u32[]{:S(2)}) collective-permute-start(bf16[32,4096]{1,0:T(8,128)(2,1)S(1)} %collective-permute-done), channel_id=1, source_target_pairs={{0,4},{4,8},{8,12},{12,16},{16,20},{20,24},{24,28},{28,0},{1,5},{5... | collective-permute-start | bytes 786440 | tf_op jit(solution)/shard_map/ppermute | solution.py:16
  21.6 8.2 %collective-permute-start.2 = (bf16[32,4096]{1,0:T(8,128)(2,1)S(1)}, bf16[32,4096]{1,0:T(8,128)(2,1)S(1)}, u32[]{:S(2)}, u32[]{:S(2)}) collective-permute-start(bf16[32,4096]{1,0:T(8,128)(2,1)S(1)} %collective-permute-done.1), channel_id=1, source_target_pairs={{0,4},{4,8},{8,12},{12,16},{16,20},{20,24},{24,28},{28,0},{1,5},{5... | collective-permute-start | bytes 786440 | tf_op jit(solution)/shard_map/ppermute | solution.py:16
  29.8 8.5 %collective-permute-start.3 = (bf16[32,4096]{1,0:T(8,128)(2,1)S(1)}, bf16[32,4096]{1,0:T(8,128)(2,1)S(1)}, u32[]{:S(2)}, u32[]{:S(2)}) collective-permute-start(bf16[32,4096]{1,0:T(8,128)(2,1)S(1)} %collective-permute-done.2), channel_id=1, source_target_pairs={{0,4},{4,8},{8,12},{12,16},{16,20},{20,24},{24,28},{28,0},{1,5},{5... | collective-permute-start | bytes 786440 | tf_op jit(solution)/shard_map/ppermute | solution.py:16
  38.3 6.7 %collective-permute-start.4 = (bf16[32,4096]{1,0:T(8,128)(2,1)S(1)}, bf16[32,4096]{1,0:T(8,128)(2,1)S(1)}, u32[]{:S(2)}, u32[]{:S(2)}) collective-permute-start(bf16[32,4096]{1,0:T(8,128)(2,1)S(1)} %collective-permute-done.3), channel_id=1, source_target_pairs={{0,4},{4,8},{8,12},{12,16},{16,20},{20,24},{24,28},{28,0},{1,5},{5... | collective-permute-start | bytes 786440 | tf_op jit(solution)/shard_map/ppermute | solution.py:16
  45.0 6.7 %collective-permute-start.5 = (bf16[32,4096]{1,0:T(8,128)(2,1)S(1)}, bf16[32,4096]{1,0:T(8,128)(2,1)S(1)}, u32[]{:S(2)}, u32[]{:S(2)}) collective-permute-start(bf16[32,4096]{1,0:T(8,128)(2,1)S(1)} %collective-permute-done.4), channel_id=1, source_target_pairs={{0,4},{4,8},{8,12},{12,16},{16,20},{20,24},{24,28},{28,0},{1,5},{5... | collective-permute-start | bytes 786440 | tf_op jit(solution)/shard_map/ppermute | solution.py:16
  51.7 6.7 %collective-permute-start.6 = (bf16[32,4096]{1,0:T(8,128)(2,1)S(1)}, bf16[32,4096]{1,0:T(8,128)(2,1)S(1)}, u32[]{:S(2)}, u32[]{:S(2)}) collective-permute-start(bf16[32,4096]{1,0:T(8,128)(2,1)S(1)} %collective-permute-done.5), channel_id=1, source_target_pairs={{0,4},{4,8},{8,12},{12,16},{16,20},{20,24},{24,28},{28,0},{1,5},{5... | collective-permute-start | bytes 786440 | tf_op jit(solution)/shard_map/ppermute | solution.py:16
  58.9 5.1 %copy-start.1 = (bf16[256,256]{1,0:T(8,128)(2,1)S(1)}, bf16[256,256]{1,0:T(8,128)(2,1)}, u32[]{:S(2)}) copy-start(bf16[256,256]{1,0:T(8,128)(2,1)} %param.7) | copy-start | bytes 393220
  58.9 5.1 %copy-start.3 = (f32[4096]{0:T(1024)S(1)}, f32[4096]{0:T(1024)}, u32[]{:S(2)}) copy-start(f32[4096]{0:T(1024)} %param.9) | copy-start | bytes 49156
Sparse Core Ops, SparseCore 0:
  10.5 33.2 all-gather.1
  88.2 49.0 reduce-scatter.1
